TPU v7x, 512 devices: a whole 4x8x8 slice. The times are simulated.
512 devices in a mesh: req: 128 (over y, z, core), tp: 4 (over x).
Axes of the slice: x: 4, y: 8, z: 8, core: 2. Of those that a mesh axis runs over, the one named last changes fastest.
Arguments:
- qkv_rows: bfloat16 [32768, 3, 1536], P('req', None, 'tp'), may hold values from -13 to 13
- row_request: int32 [32768], P('req'), may hold values from 0 to 127, as said below
- request_owner: int32 [128], replicated, may hold values from 0 to 127, each once
- cached_len: int32 [128], P('req'), may hold values from 0 to 1024
- page_table: int32 [128, 8], P('req'), may hold values from 0 to 7, as said below
- kv_pages: bfloat16 [1024, 2, 128, 1536], P('req', None, None, 'tp'), may hold values from -6 to 6
- residual: bfloat16 [32768, 3072], P('req', 'tp'), may hold values from -128 to 128
- out_weight: bfloat16 [1536, 3072], P('tp'), may hold values from -0.15625 to 0.15625
- norm_gain: bfloat16 [3072], P('tp'), may hold values from 0.5 to 1.5
Outputs:
- new_residual: bfloat16 [32768, 3072], P('req', 'tp')
- normed: bfloat16 [32768, 3072], P('req', 'tp')
Inputs may be any that keep to these rules, and one draw needn't show every extreme that they name: `row_request`: on every device at most 5 new tokens name the same request, and one request is named by exactly 5 tokens on every device. Half of the requests are named by exactly one token in all, and no two of those tokens lie on one device. `request_owner`: each device holds the cache of exactly one request. `page_table`: each row names every page of its device's pool once.
All inputs are finite; a program needn't handle non-finite values.
Results may differ from a plain program's by a relative error of at most 0.0093.
The roundings to bfloat16 on the way count: a program that leaves them out, or rounds other values in their place, can miss the bound.
Values may be sent and summed in bfloat16 or wider, within the bound.
No kernel may reach another device: no remote copies, remote signals or barrier semaphores. Data moves between devices by JAX's collectives and lax.ppermute only.
A program may use at most 64 MiB of HBM per device.

v0:
```python
import math
import jax
import jax.numpy as jnp
from jax import lax
from jax.sharding import PartitionSpec as P

D = 3072
HEAD_SIZE = 96
SLOT = 5
REQ = ("ry", "rz", "rc")
OUTER = 8
ROPE_BASE = 10000.0
EPS = 1e-05


def rope_tables(position):
    halves = HEAD_SIZE // 2
    inverse = ROPE_BASE ** (-2.0 * jnp.arange(halves, dtype=jnp.float32) / HEAD_SIZE)
    angles = position.astype(jnp.float32)[:, None] * inverse[None, :]
    cosine = jnp.concatenate([jnp.cos(angles), jnp.cos(angles)], axis=1)
    sine_tab = jnp.concatenate([jnp.sin(angles), jnp.sin(angles)], axis=1)
    return (cosine, sine_tab)


def rotate(field, cosine, sine_tab):
    halves = HEAD_SIZE // 2
    turned = jnp.concatenate([-field[..., halves:], field[..., :halves]], axis=-1)
    return field * cosine[:, None, :] + turned * sine_tab[:, None, :]


def attend_heads(grouped, cache_keys, cache_values, cosine, sine_tab, visible):
    score_scale = 1.0 / math.sqrt(HEAD_SIZE)
    query_rows_block = rotate(grouped[:, 0].astype(jnp.float32), cosine, sine_tab).astype(
        jnp.bfloat16
    )
    fresh_keys = rotate(grouped[:, 1].astype(jnp.float32), cosine, sine_tab).astype(jnp.bfloat16)
    gathered_keys = jnp.concatenate([cache_keys, fresh_keys], axis=0)
    gathered_values = jnp.concatenate([cache_values, grouped[:, 2]], axis=0)

    def one_head(head_parts):
        head_query, head_keys, head_values = head_parts
        logit_scores = (
            jnp.einsum("md,kd->mk", head_query, head_keys, preferred_element_type=jnp.float32)
            * score_scale
        )
        logit_scores = jnp.where(visible, logit_scores, -1e30)
        top_score = jnp.max(logit_scores, axis=1, keepdims=True)
        weight = jnp.exp(logit_scores - top_score)
        softmax_weights = (weight / jnp.sum(weight, axis=1, keepdims=True)).astype(jnp.bfloat16)
        return jnp.einsum(
            "mk,kd->md", softmax_weights, head_values, preferred_element_type=jnp.float32
        ).astype(jnp.bfloat16)

    heads_out = lax.map(
        one_head,
        (
            query_rows_block.transpose(1, 0, 2),
            gathered_keys.transpose(1, 0, 2),
            gathered_values.transpose(1, 0, 2),
        ),
    )
    return heads_out.transpose(1, 0, 2)


def two_stage_all_to_all(x):
    devices = x.shape[0]
    inner = devices // OUTER
    x = x.reshape((OUTER, inner) + x.shape[1:])
    x = lax.all_to_all(x, "ry", split_axis=0, concat_axis=0, tiled=True)
    x = lax.all_to_all(x, ("rz", "rc"), split_axis=1, concat_axis=1, tiled=True)
    return x.reshape((devices,) + x.shape[2:])


def on_device(
    qkv_rows,
    row_request,
    request_owner,
    cached_len,
    page_table,
    kv_pages,
    residual,
    out_weight,
    norm_gain,
):
    row_count = qkv_rows.shape[0]
    parts = qkv_rows.shape[1]
    head_cols = qkv_rows.shape[2]
    heads_here = head_cols // HEAD_SIZE
    devices = lax.axis_size(REQ)
    slot_cap = SLOT
    buffer_len = devices * slot_cap
    device_ids = jnp.arange(devices, dtype=jnp.int32)
    row_ids = jnp.arange(row_count, dtype=jnp.int32)
    owner_dev = request_owner[row_request]
    same_owner = owner_dev[:, None] == owner_dev[None, :]
    slot_in = jnp.sum(
        (same_owner & (row_ids[None, :] < row_ids[:, None])).astype(jnp.int32), axis=1
    )
    sends_to = owner_dev[:, None] == device_ids[None, :]
    counts = jnp.sum(sends_to.astype(jnp.int32), axis=0)
    pick = (
        sends_to[None, :, :]
        & (slot_in[None, :, None] == jnp.arange(slot_cap, dtype=jnp.int32)[:, None, None])
    ).astype(jnp.bfloat16)
    slots = jnp.einsum("jid,ipc->djpc", pick, qkv_rows, preferred_element_type=jnp.float32).astype(
        jnp.bfloat16
    )
    count_row = jnp.broadcast_to(
        counts.astype(jnp.bfloat16)[:, None, None], (devices, 1, head_cols)
    )
    outgoing = jnp.concatenate(
        [slots.reshape(devices, slot_cap * parts, head_cols), count_row], axis=1
    )
    arrived = two_stage_all_to_all(outgoing)
    arrived_counts = arrived[:, slot_cap * parts, 0].astype(jnp.int32)
    length = cached_len[0]
    pool_pages = kv_pages[page_table[0]]
    cache_span = pool_pages.shape[0] * pool_pages.shape[2]
    cache_keys = pool_pages[:, 0].reshape(cache_span, heads_here, HEAD_SIZE)
    cache_values = pool_pages[:, 1].reshape(cache_span, heads_here, HEAD_SIZE)
    live_slot = (jnp.arange(slot_cap, dtype=jnp.int32)[None, :] < arrived_counts[:, None]).reshape(
        buffer_len
    )
    live_int = live_slot.astype(jnp.int32)
    new_rank = jnp.cumsum(live_int) - live_int
    cosine, sine_tab = rope_tables(length + new_rank)
    cache_ok = jnp.broadcast_to(
        (jnp.arange(cache_span, dtype=jnp.int32) < length)[None, :], (buffer_len, cache_span)
    )
    new_ok = live_slot[None, :] & (new_rank[None, :] <= new_rank[:, None])
    visible = jnp.concatenate([cache_ok, new_ok], axis=1)
    grouped = arrived[:, : slot_cap * parts].reshape(buffer_len, parts, heads_here, HEAD_SIZE)
    result = attend_heads(grouped, cache_keys, cache_values, cosine, sine_tab, visible)
    returned = two_stage_all_to_all(result.reshape(devices, slot_cap * parts, head_cols // parts))
    target = owner_dev * slot_cap + slot_in
    attn_rows = returned.reshape(buffer_len, head_cols)[target]
    partial_sum = jnp.dot(attn_rows, out_weight, preferred_element_type=jnp.float32)
    mixed_cols = lax.psum_scatter(
        partial_sum.astype(jnp.bfloat16), "tp", scatter_dimension=1, tiled=True
    ).astype(jnp.float32)
    hidden = residual.astype(jnp.float32) + mixed_cols
    square_sum = lax.psum(jnp.sum(hidden * hidden, axis=1), "tp")
    inv_rms = lax.rsqrt(square_sum / D + EPS)
    normed = hidden * inv_rms[:, None] * norm_gain.astype(jnp.float32)[None, :]
    return (hidden.astype(jnp.bfloat16), normed.astype(jnp.bfloat16))


def solution(mesh):
    req_size = mesh.shape["req"]
    split_mesh = jax.sharding.Mesh(
        mesh.devices.reshape(OUTER, req_size // OUTER // 2, 2, mesh.shape["tp"]), REQ + ("tp",)
    )
    return jax.shard_map(
        on_device,
        mesh=split_mesh,
        in_specs=(
            P(REQ, None, "tp"),
            P(REQ),
            P(),
            P(REQ),
            P(REQ, None),
            P(REQ, None, None, "tp"),
            P(REQ, "tp"),
            P("tp", None),
            P("tp"),
        ),
        out_specs=(P(REQ, "tp"), P(REQ, "tp")),
        check_vma=False,
    )
```

profile of v0, /device:TPU:8, one launch (start us, length us, event | category | flops | bytes accessed | tf_op | source)
XLA Modules:
  0.0 255.4 jit_solution(9583415751893050044)
XLA Ops:
  16.2 45.9 %all_to_all.20 = bf16[8,16,16,384]{3,2,1,0:T(8,128)(2,1)S(1)} all-to-all(bf16[8,16,16,384]{3,2,1,0:T(8,128)(2,1)S(1)} %pad_maximum_fusion), channel_id=1, replica_groups=mesh['ry'=8,'rz'=8,'rc'=2,'tp'=4] {'ry'}, dimensions={0} | all-to-all | bytes 3145728 | tf_op jit(solution)/shard_map/all_to_all | solution.py:69
  63.5 10.6 %all-to-all-start.1 = ((bf16[8,16,16,384]{3,2,0,1:T(8,128)(2,1)}), bf16[8,16,16,384]{3,2,0,1:T(8,128)(2,1)}, u32[]{:S(2)}, u32[]{:S(2)}) async-start(bf16[8,16,16,384]{3,2,0,1:T(8,128)(2,1)} %copy.63), calls=%async_computation.1 | async-start | bytes 3145728 | tf_op jit(solution)/shard_map/all_to_all | solution.py:70
  74.8 3.3 %gather_fusion.1 = bf16[8,2,128,384]{3,2,1,0:T(8,128)(2,1)} fusion(bf16[8,2,128,384]{3,2,1,0:T(8,128)(2,1)} %param.16, s32[1024]{0:T(1024)S(1)} %pad_clamp_fusion.1), kind=kCustom, calls=%fused_computation.1 | custom fusion | bytes 3145760 | tf_op jit(solution)/shard_map/gather | solution.py:117
  78.1 2.8 %fusion.31 = (bf16[8,1,128,384]{3,2,1,0:T(8,128)(2,1)}, bf16[8,1,128,384]{3,2,1,0:T(8,128)(2,1)}) fusion(bf16[8,2,128,384]{3,2,1,0:T(8,128)(2,1)} %gather_fusion.1), kind=kLoop, calls=%fused_computation.78 | loop fusion | bytes 3145728 | tf_op jit(solution)/shard_map/slice | solution.py:120
  86.6 25.4 %all-to-all-done.1 = bf16[8,16,16,384]{3,2,0,1:T(8,128)(2,1)} async-done(((bf16[8,16,16,384]{3,2,0,1:T(8,128)(2,1)}), bf16[8,16,16,384]{3,2,0,1:T(8,128)(2,1)}, u32[]{:S(2)}, u32[]{:S(2)}) %all-to-all-start.1) | async-done | bytes 1572896 | tf_op jit(solution)/shard_map/all_to_all | solution.py:70
  114.7 2.4 fusion.27
  118.1 4.9 %reshape.231 = bf16[640,3,4,96]{3,2,1,0:T(4,128)(2,1)} reshape(bf16[128,15,384]{2,1,0:T(8,128)(2,1)} %bitcast.88) | data formatting | bytes 2949120 | tf_op jit(solution)/shard_map/reshape | solution.py:132
  123.0 2.7 %slice_bitcast_fusion = (bf16[640,4,96]{2,1,0:T(4,128)(2,1)}, f32[640,4,96]{2,1,0:T(4,128)S(1)}, f32[640,4,96]{2,1,0:T(4,128)S(1)}) fusion(bf16[640,3,4,96]{3,2,1,0:T(4,128)(2,1)} %reshape.231), kind=kLoop, calls=%fused_computation.38 | loop fusion | flops 491520 | bytes 3932160 | tf_op jit(solution)/shard_map/squeeze | solution.py:38
  128.7 2.7 %fusion.16 = (bf16[640,4,96]{2,1,0:T(4,128)(2,1)S(1)}, bf16[4,640,96]{2,0,1:T(4,128)(2,1)}) fusion(f32[640,4,48]{2,1,0:T(4,128)S(1)} %get-tuple-element.89, f32[640,4,48]{2,1,0:T(4,128)S(1)} %get-tuple-element.88, f32[640,96]{1,0:T(8,128)S(1)} %get-tuple-element.101, f32[640,96]{1,0:T(8,128)S(1)} %get-tuple-element.100, ...), kind=kLoop, calls=%fused_computation.31 | loop fusion | flops 2949120 | bytes 4423680 | tf_op jit(solution)/shard_map/convert_element_type | solution.py:36
  138.2 2.3 maximum_bitcast_fusion
  142.0 22.0 %while.10 = (s32[]{:T(128)}, bf16[4,640,96]{1,2,0:T(8,128)(2,1)}, bf16[4,640,96]{2,1,0:T(8,128)(2,1)}, bf16[4,1664,96]{1,2,0:T(8,128)(2,1)}, pred[640,1664]{1,0:...) while((s32[]{:T(128)}, bf16[4,640,96]{1,2,0:T(8,128)(2,1)}, bf16[4,640,96]{2,1,0:T(8,128)(2,1)}, ...), condition=%wide.region_7.8_spmd, body=%wide.region_4.7_spmd.sunk | while | flops 417524480 | bytes 14785101 | solution.py:54
  142.0 2.1 fusion.39
  144.9 2.6 %fusion.41 = bf16[4,640,96]{1,2,0:T(8,128)(2,1)} fusion(bf16[4,640,96]{1,2,0:T(8,128)(2,1)} %get-tuple-element.151, s32[]{:T(128)} %get-tuple-element.150, f32[640,1664]{1,0:T(8,128)S(1)} %get-tuple-element.141, f32[640]{0:T(1024)S(1)} %fusion.40, f32[640]{0:T(1024)S(1)} %get-tuple-element.142, bf16[4,1664,96]{1,2,0:T(8,128)(2,1)} %get-tuple-element.162), kind=kOutput, calls=%fused_computation.10.clone.1 | convolution fusion | flops 207728640 | bytes 4708352 | tf_op jit(solution)/shard_map/while/body/eval_jaxpr/mk,kd->md/dot_general | solution.py:50
  147.5 2.1 fusion.39
  150.4 2.6 %fusion.41 = bf16[4,640,96]{1,2,0:T(8,128)(2,1)} fusion(bf16[4,640,96]{1,2,0:T(8,128)(2,1)} %get-tuple-element.151, s32[]{:T(128)} %get-tuple-element.150, f32[640,1664]{1,0:T(8,128)S(1)} %get-tuple-element.141, f32[640]{0:T(1024)S(1)} %fusion.40, f32[640]{0:T(1024)S(1)} %get-tuple-element.142, bf16[4,1664,96]{1,2,0:T(8,128)(2,1)} %get-tuple-element.162), kind=kOutput, calls=%fused_computation.10.clone.1 | convolution fusion | flops 207728640 | bytes 4708352 | tf_op jit(solution)/shard_map/while/body/eval_jaxpr/mk,kd->md/dot_general | solution.py:50
  153.0 2.1 fusion.39
  155.9 2.6 %fusion.41 = bf16[4,640,96]{1,2,0:T(8,128)(2,1)} fusion(bf16[4,640,96]{1,2,0:T(8,128)(2,1)} %get-tuple-element.151, s32[]{:T(128)} %get-tuple-element.150, f32[640,1664]{1,0:T(8,128)S(1)} %get-tuple-element.141, f32[640]{0:T(1024)S(1)} %fusion.40, f32[640]{0:T(1024)S(1)} %get-tuple-element.142, bf16[4,1664,96]{1,2,0:T(8,128)(2,1)} %get-tuple-element.162), kind=kOutput, calls=%fused_computation.10.clone.1 | convolution fusion | flops 207728640 | bytes 4708352 | tf_op jit(solution)/shard_map/while/body/eval_jaxpr/mk,kd->md/dot_general | solution.py:50
  161.4 2.6 %fusion.41 = bf16[4,640,96]{1,2,0:T(8,128)(2,1)} fusion(bf16[4,640,96]{1,2,0:T(8,128)(2,1)} %get-tuple-element.151, s32[]{:T(128)} %get-tuple-element.150, f32[640,1664]{1,0:T(8,128)S(1)} %get-tuple-element.141, f32[640]{0:T(1024)S(1)} %fusion.40, f32[640]{0:T(1024)S(1)} %get-tuple-element.142, bf16[4,1664,96]{1,2,0:T(8,128)(2,1)} %get-tuple-element.162), kind=kOutput, calls=%fused_computation.10.clone.1 | convolution fusion | flops 207728640 | bytes 4708352 | tf_op jit(solution)/shard_map/while/body/eval_jaxpr/mk,kd->md/dot_general | solution.py:50
  166.5 20.6 %all_to_all.21 = bf16[8,16,15,128]{3,1,2,0:T(8,128)(2,1)S(1)} all-to-all(bf16[8,16,15,128]{3,1,2,0:T(8,128)(2,1)S(1)} %copy.74), channel_id=1, replica_groups=mesh['ry'=8,'rz'=8,'rc'=2,'tp'=4] {'ry'}, dimensions={0} | all-to-all | bytes 983040 | tf_op jit(solution)/shard_map/all_to_all | solution.py:69
  188.0 4.0 %all-to-all-start.3 = ((bf16[8,16,15,128]{3,0,2,1:T(8,128)(2,1)}), bf16[8,16,15,128]{3,0,2,1:T(8,128)(2,1)S(1)}, u32[]{:S(2)}, u32[]{:S(2)}) async-start(bf16[8,16,15,128]{3,0,2,1:T(8,128)(2,1)} %copy.75), calls=%async_computation.3 | async-start | bytes 983040 | tf_op jit(solution)/shard_map/all_to_all | solution.py:70
  192.1 15.4 %all-to-all-done.3 = bf16[8,16,15,128]{3,0,2,1:T(8,128)(2,1)S(1)} async-done(((bf16[8,16,15,128]{3,0,2,1:T(8,128)(2,1)}), bf16[8,16,15,128]{3,0,2,1:T(8,128)(2,1)S(1)}, u32[]{:S(2)}, u32[]{:S(2)}) %all-to-all-start.3) | async-done | bytes 491552 | tf_op jit(solution)/shard_map/all_to_all | solution.py:70
  209.0 2.1 convolution_convert_fusion
  211.8 24.5 %reduce-scatter.2.cloned.1.call-done = bf16[256,768]{1,0:T(8,128)(2,1)} async-done(((bf16[256,3072]{1,0:T(8,128)(2,1)}), bf16[256,768]{1,0:T(8,128)(2,1)}) %reduce-scatter.2.cloned.1.call-update) | async-done | bytes 393232 | tf_op jit(solution)/shard_map/reduce_scatter | solution.py:138
  237.5 9.1 %psum.7 = f32[256]{0:T(256)S(1)} all-reduce(f32[256]{0:T(256)S(1)} %multiply_reduce_fusion), channel_id=1, replica_groups=mesh['ry'=8,'rz'=8,'rc'=2,'tp'=4] {'tp'}, use_global_device_ids=true, to_apply=%region_10.11 | all-reduce | flops 256 | bytes 2048 | tf_op jit(solution)/shard_map/psum | solution.py:142
  (83 shorter events, 45.0 us)
Async XLA Ops:
  7.2 201.8 %copy-start = (bf16[384,3072]{1,0:T(8,128)(2,1)S(1)}, bf16[384,3072]{1,0:T(8,128)(2,1)}, u32[]{:S(2)}) copy-start(bf16[384,3072]{1,0:T(8,128)(2,1)} %param.18) | copy-start | bytes 7077892
  63.5 11.3 %copy-start.9 = (s32[1,8]{1,0:T(1,128)S(1)}, s32[1,8]{1,0:T(1,128)}, u32[]{:S(2)}) copy-start(s32[1,8]{1,0:T(1,128)} %param.15) | copy-start | bytes 100
  63.5 48.5 %all-to-all-start.1 = ((bf16[8,16,16,384]{3,2,0,1:T(8,128)(2,1)}), bf16[8,16,16,384]{3,2,0,1:T(8,128)(2,1)}, u32[]{:S(2)}, u32[]{:S(2)}) async-start(bf16[8,16,16,384]{3,2,0,1:T(8,128)(2,1)} %copy.63), calls=%async_computation.1 | async-start | bytes 3145728 | tf_op jit(solution)/shard_map/all_to_all | solution.py:70
  113.6 1.1 copy-start.2
  127.2 1.5 copy-start.1
  132.8 5.3 %copy-start.4 = (bf16[1024,4,96]{0,2,1:T(8,128)(2,1)S(1)}, bf16[1024,4,96]{0,2,1:T(8,128)(2,1)}, u32[]{:S(2)}) copy-start(bf16[1024,4,96]{0,2,1:T(8,128)(2,1)} %reshape_squeeze.6) | copy-start | bytes 2359300
  138.1 2.3 copy-start.6
  138.1 2.7 %copy-start.3 = (bf16[1024,4,96]{0,2,1:T(8,128)(2,1)S(1)}, bf16[1024,4,96]{0,2,1:T(8,128)(2,1)}, u32[]{:S(2)}) copy-start(bf16[1024,4,96]{0,2,1:T(8,128)(2,1)} %reshape_squeeze.7) | copy-start | bytes 2359300
  138.1 2.7 %copy-start.5 = (bf16[640,4,96]{0,2,1:T(8,128)(2,1)S(1)}, bf16[640,4,96]{0,2,1:T(8,128)(2,1)}, u32[]{:S(2)}) copy-start(bf16[640,4,96]{0,2,1:T(8,128)(2,1)} %copy.69) | copy-start | bytes 1474564
  188.0 19.4 %all-to-all-start.3 = ((bf16[8,16,15,128]{3,0,2,1:T(8,128)(2,1)}), bf16[8,16,15,128]{3,0,2,1:T(8,128)(2,1)S(1)}, u32[]{:S(2)}, u32[]{:S(2)}) async-start(bf16[8,16,15,128]{3,0,2,1:T(8,128)(2,1)} %copy.75), calls=%async_computation.3 | async-start | bytes 983040 | tf_op jit(solution)/shard_map/all_to_all | solution.py:70
  192.0 44.3 %reduce-scatter.2.cloned.1.call-start = ((), (), s32[]{:S(2)}) async-start(), calls=%async_computation.5 | async-start | bytes 1966080 | tf_op jit(solution)/shard_map/reduce_scatter | solution.py:138
  211.1 0.7 copy-start.8
  211.1 25.2 %copy-start.7 = (bf16[256,768]{1,0:T(8,128)(2,1)S(1)}, bf16[256,768]{1,0:T(8,128)(2,1)}, u32[]{:S(2)}) copy-start(bf16[256,768]{1,0:T(8,128)(2,1)} %param.17) | copy-start | bytes 1179652
Sparse Core Ops, SparseCore 0:
  211.3 24.9 reduce-scatter.1
where the time goes:
time: 257 us; the launch traced here: 255 us
  blocking collectives  75.5 us (29%)
  waiting for transfers between devices  65.3 us (25%)
  local copies, waits for them, and re-layouts  36.8 us (14%)
  other arithmetic  25.4 us (10%)
  matrix products  22.9 us (9%)
  between operations  15 us (6%)
  starting transfers between devices  14.6 us (6%)
    all_to_all x2, blocking collectives, two_stage_all_to_all(): x = lax.all_to_all(x, 'ry', split_axis=0, concat_axis=0, tiled=True)  66.4 us
    all_to_all x2, waiting for transfers between devices, two_stage_all_to_all(): x = lax.all_to_all(x, ('rz', 'rc'), split_axis=1, concat_axis=1, tiled=True)  40.8 us
    reduce_scatter x1, waiting for transfers between devices, on_device(): lax.psum_scatter(partial_sum.astype(jnp.bfloat16), 'tp', scatter_dimensio...  24.5 us
    all_to_all x2, starting transfers between devices, two_stage_all_to_all(): x = lax.all_to_all(x, ('rz', 'rc'), split_axis=1, concat_axis=1, tiled=True)  14.6 us
    dot_general x4, matrix products, one_head(): jnp.einsum('mk,kd->md', softmax_weights, head_values, preferred_element_t...  10.6 us
    psum x1, blocking collectives, on_device(): square_sum = lax.psum(jnp.sum(hidden * hidden, axis=1), 'tp')  9.06 us
    dot_general x4, matrix products, one_head(): jnp.einsum('md,kd->mk', head_query, head_keys, preferred_element_type=jnp...  8.57 us
  transfers between devices with their start and end apart: 3, of which 3 were waited for; matrix products, arithmetic and copies ran while one was open for 5% of the time, Pallas kernels for 0%

commit v1 on v0

--- a/solution.py
+++ b/solution.py
@@ -139,7 +139,7 @@
         partial_sum.astype(jnp.bfloat16), "tp", scatter_dimension=1, tiled=True
     ).astype(jnp.float32)
     hidden = residual.astype(jnp.float32) + mixed_cols
-    square_sum = lax.psum(jnp.sum(hidden * hidden, axis=1), "tp")
+    square_sum = lax.all_gather(jnp.sum(hidden * hidden, axis=1), "tp").sum(axis=0)
     inv_rms = lax.rsqrt(square_sum / D + EPS)
     normed = hidden * inv_rms[:, None] * norm_gain.astype(jnp.float32)[None, :]
     return (hidden.astype(jnp.bfloat16), normed.astype(jnp.bfloat16))

time: 257 us -> 256 us (level)
    psum x1 -> x0, blocking collectives: 9.06 us -> none  [on_device(): square_sum = lax.psum(jnp.sum(hidden * hidden, axis=1), 'tp')]
    all_gather x0 -> x1, blocking collectives: none -> 8.3 us  [on_device(): lax.all_gather(jnp.sum(hidden * hidden, axis=1), 'tp').sum(axis=0)]
where the time goes in v1:
time: 256 us; the launch traced here: 255 us
  blocking collectives  74.7 us (29%)
  waiting for transfers between devices  65.3 us (26%)
  local copies, waits for them, and re-layouts  36.8 us (14%)
  other arithmetic  25.4 us (10%)
  matrix products  22.9 us (9%)
  between operations  15 us (6%)
  starting transfers between devices  14.6 us (6%)
    all_to_all x2, blocking collectives, two_stage_all_to_all(): x = lax.all_to_all(x, 'ry', split_axis=0, concat_axis=0, tiled=True)  66.4 us
    all_to_all x2, waiting for transfers between devices, two_stage_all_to_all(): x = lax.all_to_all(x, ('rz', 'rc'), split_axis=1, concat_axis=1, tiled=True)  40.8 us
    reduce_scatter x1, waiting for transfers between devices, on_device(): lax.psum_scatter(partial_sum.astype(jnp.bfloat16), 'tp', scatter_dimensio...  24.5 us
    all_to_all x2, starting transfers between devices, two_stage_all_to_all(): x = lax.all_to_all(x, ('rz', 'rc'), split_axis=1, concat_axis=1, tiled=True)  14.6 us
    dot_general x4, matrix products, one_head(): jnp.einsum('mk,kd->md', softmax_weights, head_values, preferred_element_t...  10.6 us
    dot_general x4, matrix products, one_head(): jnp.einsum('md,kd->mk', head_query, head_keys, preferred_element_type=jnp...  8.57 us
    all_gather x1, blocking collectives, on_device(): lax.all_gather(jnp.sum(hidden * hidden, axis=1), 'tp').sum(axis=0)  8.3 us
  transfers between devices with their start and end apart: 3, of which 3 were waited for; matrix products, arithmetic and copies ran while one was open for 5% of the time, Pallas kernels for 0%

profile of v1, /device:TPU:8, one launch (start us, length us, event | category | flops | bytes accessed | tf_op | source)
XLA Modules:
  0.0 254.7 jit_solution(7145584580966698751)
XLA Ops:
  16.2 45.9 %all_to_all.20 = bf16[8,16,16,384]{3,2,1,0:T(8,128)(2,1)S(1)} all-to-all(bf16[8,16,16,384]{3,2,1,0:T(8,128)(2,1)S(1)} %pad_maximum_fusion), channel_id=1, replica_groups=mesh['ry'=8,'rz'=8,'rc'=2,'tp'=4] {'ry'}, dimensions={0} | all-to-all | bytes 3145728 | tf_op jit(solution)/shard_map/all_to_all | solution.py:69
  63.5 10.6 %all-to-all-start.1 = ((bf16[8,16,16,384]{3,2,0,1:T(8,128)(2,1)}), bf16[8,16,16,384]{3,2,0,1:T(8,128)(2,1)}, u32[]{:S(2)}, u32[]{:S(2)}) async-start(bf16[8,16,16,384]{3,2,0,1:T(8,128)(2,1)} %copy.63), calls=%async_computation.1 | async-start | bytes 3145728 | tf_op jit(solution)/shard_map/all_to_all | solution.py:70
  74.8 3.3 %gather_fusion.1 = bf16[8,2,128,384]{3,2,1,0:T(8,128)(2,1)} fusion(bf16[8,2,128,384]{3,2,1,0:T(8,128)(2,1)} %param.16, s32[1024]{0:T(1024)S(1)} %pad_clamp_fusion.1), kind=kCustom, calls=%fused_computation.1 | custom fusion | bytes 3145760 | tf_op jit(solution)/shard_map/gather | solution.py:117
  78.1 2.8 %fusion.31 = (bf16[8,1,128,384]{3,2,1,0:T(8,128)(2,1)}, bf16[8,1,128,384]{3,2,1,0:T(8,128)(2,1)}) fusion(bf16[8,2,128,384]{3,2,1,0:T(8,128)(2,1)} %gather_fusion.1), kind=kLoop, calls=%fused_computation.78 | loop fusion | bytes 3145728 | tf_op jit(solution)/shard_map/slice | solution.py:120
  86.6 25.4 %all-to-all-done.1 = bf16[8,16,16,384]{3,2,0,1:T(8,128)(2,1)} async-done(((bf16[8,16,16,384]{3,2,0,1:T(8,128)(2,1)}), bf16[8,16,16,384]{3,2,0,1:T(8,128)(2,1)}, u32[]{:S(2)}, u32[]{:S(2)}) %all-to-all-start.1) | async-done | bytes 1572896 | tf_op jit(solution)/shard_map/all_to_all | solution.py:70
  114.7 2.4 fusion.27
  118.1 4.9 %reshape.235 = bf16[640,3,4,96]{3,2,1,0:T(4,128)(2,1)} reshape(bf16[128,15,384]{2,1,0:T(8,128)(2,1)} %bitcast.89) | data formatting | bytes 2949120 | tf_op jit(solution)/shard_map/reshape | solution.py:132
  123.0 2.7 %slice_bitcast_fusion = (bf16[640,4,96]{2,1,0:T(4,128)(2,1)}, f32[640,4,96]{2,1,0:T(4,128)S(1)}, f32[640,4,96]{2,1,0:T(4,128)S(1)}) fusion(bf16[640,3,4,96]{3,2,1,0:T(4,128)(2,1)} %reshape.235), kind=kLoop, calls=%fused_computation.38 | loop fusion | flops 491520 | bytes 3932160 | tf_op jit(solution)/shard_map/squeeze | solution.py:38
  128.7 2.7 %fusion.16 = (bf16[640,4,96]{2,1,0:T(4,128)(2,1)S(1)}, bf16[4,640,96]{2,0,1:T(4,128)(2,1)}) fusion(f32[640,4,48]{2,1,0:T(4,128)S(1)} %get-tuple-element.89, f32[640,4,48]{2,1,0:T(4,128)S(1)} %get-tuple-element.88, f32[640,96]{1,0:T(8,128)S(1)} %get-tuple-element.101, f32[640,96]{1,0:T(8,128)S(1)} %get-tuple-element.100, ...), kind=kLoop, calls=%fused_computation.31 | loop fusion | flops 2949120 | bytes 4423680 | tf_op jit(solution)/shard_map/convert_element_type | solution.py:36
  138.2 2.3 maximum_bitcast_fusion
  142.0 22.0 %while.10 = (s32[]{:T(128)}, bf16[4,640,96]{1,2,0:T(8,128)(2,1)}, bf16[4,640,96]{2,1,0:T(8,128)(2,1)}, bf16[4,1664,96]{1,2,0:T(8,128)(2,1)}, pred[640,1664]{1,0:...) while((s32[]{:T(128)}, bf16[4,640,96]{1,2,0:T(8,128)(2,1)}, bf16[4,640,96]{2,1,0:T(8,128)(2,1)}, ...), condition=%wide.region_7.8_spmd, body=%wide.region_4.7_spmd.sunk | while | flops 417524480 | bytes 14785101 | solution.py:54
  142.0 2.1 fusion.39
  144.9 2.6 %fusion.41 = bf16[4,640,96]{1,2,0:T(8,128)(2,1)} fusion(bf16[4,640,96]{1,2,0:T(8,128)(2,1)} %get-tuple-element.151, s32[]{:T(128)} %get-tuple-element.150, f32[640,1664]{1,0:T(8,128)S(1)} %get-tuple-element.141, f32[640]{0:T(1024)S(1)} %fusion.40, f32[640]{0:T(1024)S(1)} %get-tuple-element.142, bf16[4,1664,96]{1,2,0:T(8,128)(2,1)} %get-tuple-element.162), kind=kOutput, calls=%fused_computation.10.clone.1 | convolution fusion | flops 207728640 | bytes 4708352 | tf_op jit(solution)/shard_map/while/body/eval_jaxpr/mk,kd->md/dot_general | solution.py:50
  147.5 2.1 fusion.39
  150.4 2.6 %fusion.41 = bf16[4,640,96]{1,2,0:T(8,128)(2,1)} fusion(bf16[4,640,96]{1,2,0:T(8,128)(2,1)} %get-tuple-element.151, s32[]{:T(128)} %get-tuple-element.150, f32[640,1664]{1,0:T(8,128)S(1)} %get-tuple-element.141, f32[640]{0:T(1024)S(1)} %fusion.40, f32[640]{0:T(1024)S(1)} %get-tuple-element.142, bf16[4,1664,96]{1,2,0:T(8,128)(2,1)} %get-tuple-element.162), kind=kOutput, calls=%fused_computation.10.clone.1 | convolution fusion | flops 207728640 | bytes 4708352 | tf_op jit(solution)/shard_map/while/body/eval_jaxpr/mk,kd->md/dot_general | solution.py:50
  153.0 2.1 fusion.39
  155.9 2.6 %fusion.41 = bf16[4,640,96]{1,2,0:T(8,128)(2,1)} fusion(bf16[4,640,96]{1,2,0:T(8,128)(2,1)} %get-tuple-element.151, s32[]{:T(128)} %get-tuple-element.150, f32[640,1664]{1,0:T(8,128)S(1)} %get-tuple-element.141, f32[640]{0:T(1024)S(1)} %fusion.40, f32[640]{0:T(1024)S(1)} %get-tuple-element.142, bf16[4,1664,96]{1,2,0:T(8,128)(2,1)} %get-tuple-element.162), kind=kOutput, calls=%fused_computation.10.clone.1 | convolution fusion | flops 207728640 | bytes 4708352 | tf_op jit(solution)/shard_map/while/body/eval_jaxpr/mk,kd->md/dot_general | solution.py:50
  161.4 2.6 %fusion.41 = bf16[4,640,96]{1,2,0:T(8,128)(2,1)} fusion(bf16[4,640,96]{1,2,0:T(8,128)(2,1)} %get-tuple-element.151, s32[]{:T(128)} %get-tuple-element.150, f32[640,1664]{1,0:T(8,128)S(1)} %get-tuple-element.141, f32[640]{0:T(1024)S(1)} %fusion.40, f32[640]{0:T(1024)S(1)} %get-tuple-element.142, bf16[4,1664,96]{1,2,0:T(8,128)(2,1)} %get-tuple-element.162), kind=kOutput, calls=%fused_computation.10.clone.1 | convolution fusion | flops 207728640 | bytes 4708352 | tf_op jit(solution)/shard_map/while/body/eval_jaxpr/mk,kd->md/dot_general | solution.py:50
  166.5 20.6 %all_to_all.21 = bf16[8,16,15,128]{3,1,2,0:T(8,128)(2,1)S(1)} all-to-all(bf16[8,16,15,128]{3,1,2,0:T(8,128)(2,1)S(1)} %copy.74), channel_id=1, replica_groups=mesh['ry'=8,'rz'=8,'rc'=2,'tp'=4] {'ry'}, dimensions={0} | all-to-all | bytes 983040 | tf_op jit(solution)/shard_map/all_to_all | solution.py:69
  188.0 4.0 %all-to-all-start.3 = ((bf16[8,16,15,128]{3,0,2,1:T(8,128)(2,1)}), bf16[8,16,15,128]{3,0,2,1:T(8,128)(2,1)S(1)}, u32[]{:S(2)}, u32[]{:S(2)}) async-start(bf16[8,16,15,128]{3,0,2,1:T(8,128)(2,1)} %copy.75), calls=%async_computation.3 | async-start | bytes 983040 | tf_op jit(solution)/shard_map/all_to_all | solution.py:70
  192.1 15.4 %all-to-all-done.3 = bf16[8,16,15,128]{3,0,2,1:T(8,128)(2,1)S(1)} async-done(((bf16[8,16,15,128]{3,0,2,1:T(8,128)(2,1)}), bf16[8,16,15,128]{3,0,2,1:T(8,128)(2,1)S(1)}, u32[]{:S(2)}, u32[]{:S(2)}) %all-to-all-start.3) | async-done | bytes 491552 | tf_op jit(solution)/shard_map/all_to_all | solution.py:70
  209.0 2.1 convolution_convert_fusion
  211.8 24.5 %reduce-scatter.2.cloned.1.call-done = bf16[256,768]{1,0:T(8,128)(2,1)} async-done(((bf16[256,3072]{1,0:T(8,128)(2,1)}), bf16[256,768]{1,0:T(8,128)(2,1)}) %reduce-scatter.2.cloned.1.call-update) | async-done | bytes 393232 | tf_op jit(solution)/shard_map/reduce_scatter | solution.py:138
  237.5 8.3 %all-gather.1 = f32[4,1,256]{2,1,0:T(1,128)S(1)} all-gather(f32[1,1,256]{2,1,0:T(1,128)S(1)} %bitcast.91), channel_id=2, replica_groups=mesh['ry'=8,'rz'=8,'rc'=2,'tp'=4] {'tp'}, dimensions={0}, use_global_device_ids=true | all-gather | bytes 5120 | tf_op jit(solution)/shard_map/all_gather | solution.py:142
  (84 shorter events, 45.1 us)
Async XLA Ops:
  7.2 201.8 %copy-start = (bf16[384,3072]{1,0:T(8,128)(2,1)S(1)}, bf16[384,3072]{1,0:T(8,128)(2,1)}, u32[]{:S(2)}) copy-start(bf16[384,3072]{1,0:T(8,128)(2,1)} %param.18) | copy-start | bytes 7077892
  63.5 11.3 %copy-start.9 = (s32[1,8]{1,0:T(1,128)S(1)}, s32[1,8]{1,0:T(1,128)}, u32[]{:S(2)}) copy-start(s32[1,8]{1,0:T(1,128)} %param.15) | copy-start | bytes 100
  63.5 48.5 %all-to-all-start.1 = ((bf16[8,16,16,384]{3,2,0,1:T(8,128)(2,1)}), bf16[8,16,16,384]{3,2,0,1:T(8,128)(2,1)}, u32[]{:S(2)}, u32[]{:S(2)}) async-start(bf16[8,16,16,384]{3,2,0,1:T(8,128)(2,1)} %copy.63), calls=%async_computation.1 | async-start | bytes 3145728 | tf_op jit(solution)/shard_map/all_to_all | solution.py:70
  113.6 1.1 copy-start.2
  127.2 1.5 copy-start.1
  132.8 5.3 %copy-start.4 = (bf16[1024,4,96]{0,2,1:T(8,128)(2,1)S(1)}, bf16[1024,4,96]{0,2,1:T(8,128)(2,1)}, u32[]{:S(2)}) copy-start(bf16[1024,4,96]{0,2,1:T(8,128)(2,1)} %reshape_squeeze.6) | copy-start | bytes 2359300
  138.1 2.3 copy-start.6
  138.1 2.7 %copy-start.3 = (bf16[1024,4,96]{0,2,1:T(8,128)(2,1)S(1)}, bf16[1024,4,96]{0,2,1:T(8,128)(2,1)}, u32[]{:S(2)}) copy-start(bf16[1024,4,96]{0,2,1:T(8,128)(2,1)} %reshape_squeeze.7) | copy-start | bytes 2359300
  138.1 2.7 %copy-start.5 = (bf16[640,4,96]{0,2,1:T(8,128)(2,1)S(1)}, bf16[640,4,96]{0,2,1:T(8,128)(2,1)}, u32[]{:S(2)}) copy-start(bf16[640,4,96]{0,2,1:T(8,128)(2,1)} %copy.69) | copy-start | bytes 1474564
  188.0 19.4 %all-to-all-start.3 = ((bf16[8,16,15,128]{3,0,2,1:T(8,128)(2,1)}), bf16[8,16,15,128]{3,0,2,1:T(8,128)(2,1)S(1)}, u32[]{:S(2)}, u32[]{:S(2)}) async-start(bf16[8,16,15,128]{3,0,2,1:T(8,128)(2,1)} %copy.75), calls=%async_computation.3 | async-start | bytes 983040 | tf_op jit(solution)/shard_map/all_to_all | solution.py:70
  192.0 44.3 %reduce-scatter.2.cloned.1.call-start = ((), (), s32[]{:S(2)}) async-start(), calls=%async_computation.5 | async-start | bytes 1966080 | tf_op jit(solution)/shard_map/reduce_scatter | solution.py:138
  211.1 0.7 copy-start.8
  211.1 25.2 %copy-start.7 = (bf16[256,768]{1,0:T(8,128)(2,1)S(1)}, bf16[256,768]{1,0:T(8,128)(2,1)}, u32[]{:S(2)}) copy-start(bf16[256,768]{1,0:T(8,128)(2,1)} %param.17) | copy-start | bytes 1179652
Sparse Core Ops, SparseCore 0:
  211.3 24.9 reduce-scatter.1
